TPU v7x, 256 devices: a whole 4x4x8 slice. The times are simulated.
256 devices in a mesh: row: 8 (over x_hi, y), feat: 32 (over x_lo, z, core).
Axes of the slice: x: 4 (x_hi: 2, x_lo: 2; x = x_hi * 2 + x_lo), y: 4, z: 8, core: 2. Of those that a mesh axis runs over, the one named last changes fastest.
Arguments:
- node_features: bfloat16 [1024, 65536], P('feat', 'row'), may hold values from -6 to 6
- adjacency: bfloat16 [2048, 128, 128], P('row'), may hold values from -0.5 to 0.5
- tile_row: int32 [2048], P('row'), may hold values from 0 to 63
- tile_col: int32 [2048], P('row'), may hold values from 0 to 63
- tile_count: int32 [8, 8], P('row'), may hold values from 1 to 32, as said below
- weight: bfloat16 [1024, 1024], P('feat'), may hold values from -0.1875 to 0.1875
- out_bias: float32 [1024], replicated, may hold values from -3 to 3
Outputs:
- activated: bfloat16 [1024, 65536], P('feat', 'row')
Inputs may be any that keep to these rules, and one draw needn't show every extreme that they name: tile_count[r, s] is at least 1; the entry with s equal to r is 32.
All inputs are finite; a program needn't handle non-finite values.
Results may differ from a plain program's by a relative error of at most 0.0095.
Values may be sent and summed in bfloat16 or wider, within the bound.
No kernel may reach another device: no remote copies, remote signals or barrier semaphores. Data moves between devices by JAX's collectives and lax.ppermute only.
A program may use at most 128 MiB of HBM per device.

v0:
```python
import jax
import jax.numpy as jnp
from jax import lax
from jax.sharding import PartitionSpec as P


def from_behind(value, axis, steps):
    count = lax.axis_size(axis)
    pairs = [(source, (source + steps) % count) for source in range(count)]
    return lax.ppermute(value, axis, pairs)


def on_device(node_features, adjacency, tile_row, tile_col, tile_count, weight, out_bias):
    feat_width = node_features.shape[0]
    rows_here = node_features.shape[1]
    tile_size = adjacency.shape[1]
    row_blocks = rows_here // tile_size
    slot_total = tile_row.shape[0] // lax.axis_size("row")
    cycle_len = lax.axis_size("row")
    own_row = lax.axis_index("row")
    counts_here = tile_count[0]
    block_ids = jnp.arange(row_blocks)
    slot_ids = jnp.arange(slot_total)

    def add_source(running, held_block, source):
        first_slot = source * slot_total
        tiles_part = lax.dynamic_slice_in_dim(adjacency, first_slot, slot_total, 0)
        rows_part = lax.dynamic_slice_in_dim(tile_row, first_slot, slot_total, 0)
        cols_part = lax.dynamic_slice_in_dim(tile_col, first_slot, slot_total, 0)
        live_count = lax.dynamic_index_in_dim(counts_here, source, 0, keepdims=False)
        blocks = held_block.reshape(feat_width, row_blocks, tile_size)
        picked = jnp.take(blocks, cols_part, axis=1)
        product = jnp.einsum("fsj,sji->fsi", picked, tiles_part, preferred_element_type=jnp.float32)
        live_mask = slot_ids < live_count
        onehot = ((rows_part[:, None] == block_ids[None, :]) & live_mask[:, None]).astype(
            jnp.float32
        )
        return running + jnp.einsum("fsi,sr->fri", product, onehot)

    running = jnp.zeros((feat_width, row_blocks, tile_size), jnp.float32)
    running = add_source(running, node_features, own_row)
    held_block = node_features
    for step_num in range(1, cycle_len):
        held_block = from_behind(held_block, "row", 1)
        running = add_source(running, held_block, (own_row - step_num) % cycle_len)
    aggregated = running.reshape(feat_width, rows_here).astype(jnp.bfloat16)
    pre_act = jnp.dot(
        weight,
        lax.all_gather(aggregated, "feat", axis=0, tiled=True),
        preferred_element_type=jnp.float32,
    )
    bias_here = lax.dynamic_slice_in_dim(
        out_bias, lax.axis_index("feat") * feat_width, feat_width, 0
    )
    activated = jax.nn.relu(pre_act + bias_here[:, None]).astype(jnp.bfloat16)
    return activated


def solution(mesh):
    in_specs = (
        P("feat", "row"),
        P("row", None, None),
        P("row"),
        P("row"),
        P("row", None),
        P("feat", None),
        P(),
    )
    out_specs = P("feat", "row")
    return jax.shard_map(
        on_device, mesh=mesh, in_specs=in_specs, out_specs=out_specs, check_vma=False
    )
```

profile of v0, /device:TPU:1, one launch (start us, length us, event | category | flops | bytes accessed | tf_op | source)
XLA Modules:
  0.0 232.1 jit_solution(2701987297199606596)
XLA Ops:
  6.5 0.0 copy-start
  6.5 0.0 all-gather.2.cloned.1.call-start
  6.5 2.1 collective-permute-start
  8.7 1.2 copy_bitcast_fusion.8
  9.9 1.7 constant_dynamic-slice_fusion
  11.5 0.6 iota_compare_fusion.8
  12.2 0.6 iota_compare_fusion.10
  12.7 0.6 iota_compare_fusion.11
  13.4 0.6 iota_compare_fusion.12
  14.0 0.6 iota_compare_fusion.13
  14.7 0.5 iota_compare_fusion.14
  15.2 0.7 iota_compare_fusion.15
  16.0 1.1 fusion.109
  17.0 1.1 compare_and_fusion
  18.2 0.7 iota_compare_fusion.9
  18.9 0.6 gather_fusion
  19.5 1.7 convolution_bitcast_fusion.7
  21.2 0.4 fusion.19
  21.6 0.9 collective-permute-done
  22.5 0.5 collective-permute-start.1
  23.0 0.1 copy_bitcast_fusion.7
  23.1 0.6 gather_fusion.1
  23.7 1.7 convolution_bitcast_fusion.6
  25.4 0.4 convolution_add_fusion.7
  25.8 10.7 %collective-permute-done.1 = bf16[32,8192]{1,0:T(8,128)(2,1)S(1)} collective-permute-done((bf16[32,8192]{1,0:T(8,128)(2,1)S(1)}, bf16[32,8192]{1,0:T(8,128)(2,1)S(1)}, u32[]{:S(2)}, u32[]{:S(2)}) %collective-permute-start.1) | collective-permute-done | bytes 524320 | tf_op jit(solution)/shard_map/ppermute | solution.py:10
  36.5 0.0 collective-permute-start.2
  36.5 0.1 copy_bitcast_fusion.6
  36.6 0.6 gather_fusion.2
  37.2 1.7 convolution_bitcast_fusion.5
  38.9 0.4 convolution_add_fusion.6
  39.3 10.3 %collective-permute-done.2 = bf16[32,8192]{1,0:T(8,128)(2,1)S(1)} collective-permute-done((bf16[32,8192]{1,0:T(8,128)(2,1)S(1)}, bf16[32,8192]{1,0:T(8,128)(2,1)S(1)}, u32[]{:S(2)}, u32[]{:S(2)}) %collective-permute-start.2) | collective-permute-done | bytes 524320 | tf_op jit(solution)/shard_map/ppermute | solution.py:10
  49.6 0.0 collective-permute-start.3
  49.6 0.1 copy_bitcast_fusion.5
  49.7 0.6 gather_fusion.3
  50.3 1.7 convolution_bitcast_fusion.4
  52.0 0.4 convolution_add_fusion.5
  52.4 9.5 %collective-permute-done.3 = bf16[32,8192]{1,0:T(8,128)(2,1)S(1)} collective-permute-done((bf16[32,8192]{1,0:T(8,128)(2,1)S(1)}, bf16[32,8192]{1,0:T(8,128)(2,1)S(1)}, u32[]{:S(2)}, u32[]{:S(2)}) %collective-permute-start.3) | collective-permute-done | bytes 524320 | tf_op jit(solution)/shard_map/ppermute | solution.py:10
  61.9 0.0 collective-permute-start.4
  61.9 0.1 copy_bitcast_fusion.4
  62.0 0.6 gather_fusion.4
  62.6 1.7 convolution_bitcast_fusion.3
  64.3 0.4 convolution_add_fusion.4
  64.7 8.8 %collective-permute-done.4 = bf16[32,8192]{1,0:T(8,128)(2,1)S(1)} collective-permute-done((bf16[32,8192]{1,0:T(8,128)(2,1)S(1)}, bf16[32,8192]{1,0:T(8,128)(2,1)S(1)}, u32[]{:S(2)}, u32[]{:S(2)}) %collective-permute-start.4) | collective-permute-done | bytes 524320 | tf_op jit(solution)/shard_map/ppermute | solution.py:10
  73.5 0.0 collective-permute-start.5
  73.5 0.1 copy_bitcast_fusion.3
  73.6 0.6 gather_fusion.5
  74.2 1.7 convolution_bitcast_fusion.2
  75.9 0.4 convolution_add_fusion.3
  76.3 9.0 %collective-permute-done.5 = bf16[32,8192]{1,0:T(8,128)(2,1)S(1)} collective-permute-done((bf16[32,8192]{1,0:T(8,128)(2,1)S(1)}, bf16[32,8192]{1,0:T(8,128)(2,1)S(1)}, u32[]{:S(2)}, u32[]{:S(2)}) %collective-permute-start.5) | collective-permute-done | bytes 524320 | tf_op jit(solution)/shard_map/ppermute | solution.py:10
  85.3 0.0 collective-permute-start.6
  85.3 0.1 copy_bitcast_fusion.2
  85.4 0.6 gather_fusion.6
  86.0 1.7 convolution_bitcast_fusion.1
  87.7 0.4 convolution_add_fusion.2
  88.1 10.1 %collective-permute-done.6 = bf16[32,8192]{1,0:T(8,128)(2,1)S(1)} collective-permute-done((bf16[32,8192]{1,0:T(8,128)(2,1)S(1)}, bf16[32,8192]{1,0:T(8,128)(2,1)S(1)}, u32[]{:S(2)}, u32[]{:S(2)}) %collective-permute-start.6) | collective-permute-done | bytes 524320 | tf_op jit(solution)/shard_map/ppermute | solution.py:10
  98.2 0.1 copy_bitcast_fusion.1
  98.3 0.6 gather_fusion.7
  98.9 1.7 convolution_bitcast_fusion
  100.6 0.4 fusion.3
  101.0 1.1 copy.58
  102.2 0.0 all-gather.2.cloned.1.call-update
  102.2 0.8 dynamic_slice.132
  102.9 112.8 %all-gather.2.cloned.1.call-done = bf16[1024,8192]{1,0:T(8,128)(2,1)} async-done(((bf16[32,8192]{1,0:T(8,128)(2,1)}), bf16[1024,8192]{1,0:T(8,128)(2,1)}) %all-gather.2.cloned.1.call-update) | async-done | bytes 16777232 | tf_op jit(solution)/shard_map/all_gather | solution.py:49
  215.8 9.6 %fusion.2 = bf16[32,8192]{1,0:T(8,128)(2,1)} fusion(bf16[32,1024]{1,0:T(8,128)(2,1)S(1)} %copy-done, bf16[1024,8192]{1,0:T(8,128)(2,1)} %all-gather.2.cloned.1.call-done, f32[32]{0:T(128)S(1)} %dynamic_slice.132), kind=kOutput, calls=%fused_computation.11 | convolution fusion | flops 537657344 | bytes 17367168 | tf_op jit(solution)/shard_map/dot_general | solution.py:47
  (9 shorter events, 0.0 us)
Async XLA Ops:
  6.5 209.2 %copy-start = (bf16[32,1024]{1,0:T(8,128)(2,1)S(1)}, bf16[32,1024]{1,0:T(8,128)(2,1)}, u32[]{:S(2)}) copy-start(bf16[32,1024]{1,0:T(8,128)(2,1)} %param.14) | copy-start | bytes 196612
  6.5 209.2 %all-gather.2.cloned.1.call-start = ((), (), s32[]{:S(2)}) async-start(), calls=%async_computation | async-start | bytes 17301504 | tf_op jit(solution)/shard_map/all_gather | solution.py:49
  6.5 16.0 %collective-permute-start = (bf16[32,8192]{1,0:T(8,128)(2,1)}, bf16[32,8192]{1,0:T(8,128)(2,1)S(1)}, u32[]{:S(2)}, u32[]{:S(2)}) collective-permute-start(bf16[32,8192]{1,0:T(8,128)(2,1)} %param.9), channel_id=1, source_target_pairs={{0,32},{32,64},{64,96},{96,128},{128,160},{160,192},{192,224},{224... | collective-permute-start | bytes 1572872 | tf_op jit(solution)/shard_map/ppermute | solution.py:10
  22.5 14.0 %collective-permute-start.1 = (bf16[32,8192]{1,0:T(8,128)(2,1)S(1)}, bf16[32,8192]{1,0:T(8,128)(2,1)S(1)}, u32[]{:S(2)}, u32[]{:S(2)}) collective-permute-start(bf16[32,8192]{1,0:T(8,128)(2,1)S(1)} %collective-permute-done), channel_id=1, source_target_pairs={{0,32},{32,64},{64,96},{96,128},{128,160},{160,192},{192,224},{224... | collective-permute-start | bytes 1572872 | tf_op jit(solution)/shard_map/ppermute | solution.py:10
  36.5 13.1 %collective-permute-start.2 = (bf16[32,8192]{1,0:T(8,128)(2,1)S(1)}, bf16[32,8192]{1,0:T(8,128)(2,1)S(1)}, u32[]{:S(2)}, u32[]{:S(2)}) collective-permute-start(bf16[32,8192]{1,0:T(8,128)(2,1)S(1)} %collective-permute-done.1), channel_id=1, source_target_pairs={{0,32},{32,64},{64,96},{96,128},{128,160},{160,192},{192,224},{224... | collective-permute-start | bytes 1572872 | tf_op jit(solution)/shard_map/ppermute | solution.py:10
  49.6 12.3 %collective-permute-start.3 = (bf16[32,8192]{1,0:T(8,128)(2,1)S(1)}, bf16[32,8192]{1,0:T(8,128)(2,1)S(1)}, u32[]{:S(2)}, u32[]{:S(2)}) collective-permute-start(bf16[32,8192]{1,0:T(8,128)(2,1)S(1)} %collective-permute-done.2), channel_id=1, source_target_pairs={{0,32},{32,64},{64,96},{96,128},{128,160},{160,192},{192,224},{224... | collective-permute-start | bytes 1572872 | tf_op jit(solution)/shard_map/ppermute | solution.py:10
  61.9 11.6 %collective-permute-start.4 = (bf16[32,8192]{1,0:T(8,128)(2,1)S(1)}, bf16[32,8192]{1,0:T(8,128)(2,1)S(1)}, u32[]{:S(2)}, u32[]{:S(2)}) collective-permute-start(bf16[32,8192]{1,0:T(8,128)(2,1)S(1)} %collective-permute-done.3), channel_id=1, source_target_pairs={{0,32},{32,64},{64,96},{96,128},{128,160},{160,192},{192,224},{224... | collective-permute-start | bytes 1572872 | tf_op jit(solution)/shard_map/ppermute | solution.py:10
  73.5 11.8 %collective-permute-start.5 = (bf16[32,8192]{1,0:T(8,128)(2,1)S(1)}, bf16[32,8192]{1,0:T(8,128)(2,1)S(1)}, u32[]{:S(2)}, u32[]{:S(2)}) collective-permute-start(bf16[32,8192]{1,0:T(8,128)(2,1)S(1)} %collective-permute-done.4), channel_id=1, source_target_pairs={{0,32},{32,64},{64,96},{96,128},{128,160},{160,192},{192,224},{224... | collective-permute-start | bytes 1572872 | tf_op jit(solution)/shard_map/ppermute | solution.py:10
  85.3 12.9 %collective-permute-start.6 = (bf16[32,8192]{1,0:T(8,128)(2,1)S(1)}, bf16[32,8192]{1,0:T(8,128)(2,1)S(1)}, u32[]{:S(2)}, u32[]{:S(2)}) collective-permute-start(bf16[32,8192]{1,0:T(8,128)(2,1)S(1)} %collective-permute-done.5), channel_id=1, source_target_pairs={{0,32},{32,64},{64,96},{96,128},{128,160},{160,192},{192,224},{224... | collective-permute-start | bytes 1572872 | tf_op jit(solution)/shard_map/ppermute | solution.py:10
Sparse Core Ops, SparseCore 0:
  102.3 113.4 all-gather.1
where the time goes:
time: 233 us; the launch traced here: 232 us
  waiting for transfers between devices  172 us (74%)
  matrix products  26.3 us (11%)
  between operations  13.8 us (6%)
  local copies, waits for them, and re-layouts  11.2 us (5%)
  other arithmetic  6.17 us (3%)
  starting transfers between devices  2.62 us (1%)
    all_gather x1, waiting for transfers between devices, on_device(): lax.all_gather(aggregated, 'feat', axis=0, tiled=True)  113 us
    ppermute x7, waiting for transfers between devices, from_behind(): return lax.ppermute(value, axis, pairs)  59.2 us
    dot_general x8, matrix products, add_source(): jnp.einsum('fsj,sji->fsi', picked, tiles_part, preferred_element_type=jnp...  13.3 us
    dot_general x1, matrix products, on_device(): jnp.dot(weight, lax.all_gather(aggregated, 'feat', axis=0, tiled=True), p...  9.55 us
    lt x8, other arithmetic, add_source(): live_mask = slot_ids < live_count  5.05 us
    gather x8, local copies, waits for them, and re-layouts, add_source(): picked = jnp.take(blocks, cols_part, axis=1)  4.82 us
  transfers between devices with their start and end apart: 8, of which 8 were waited for; matrix products, arithmetic and copies ran while one was open for 13% of the time, Pallas kernels for 0%

commit v1 on v0

--- a/solution.py
+++ b/solution.py
@@ -46,7 +46,12 @@
     aggregated = running.reshape(feat_width, rows_here).astype(jnp.bfloat16)
     pre_act = jnp.dot(
         weight,
-        lax.all_gather(aggregated, "feat", axis=0, tiled=True),
+        jnp.concatenate(
+            lax.all_to_all(
+                jnp.stack([aggregated for _ in range(lax.psum(1, "feat"))]), "feat", 0, 0
+            ),
+            axis=0,
+        ),
         preferred_element_type=jnp.float32,
     )
     bias_here = lax.dynamic_slice_in_dim(

time: 233 us -> 505 us (2.17); the launches traced: 232 us -> 495 us
  waiting for transfers between devices: 172 us -> 420 us
  starting transfers between devices: 2.62 us -> 25.8 us
  between operations: 13.8 us -> 0.42 us
  local copies, waits for them, and re-layouts: 11.2 us -> 16.4 us
    all_to_all x0 -> x1, waiting for transfers between devices: none -> 360 us  [on_device(): lax.all_to_all(jnp.stack([aggregated for _ in range(lax.psum(1, 'feat'))]...]
    all_gather x1 -> x0, waiting for transfers between devices: 113 us -> none  [on_device(): lax.all_gather(aggregated, 'feat', axis=0, tiled=True)]
    all_to_all x0 -> x1, starting transfers between devices: none -> 23.3 us  [on_device(): lax.all_to_all(jnp.stack([aggregated for _ in range(lax.psum(1, 'feat'))]...]
    another operation x0 -> x1, local copies, waits for them, and re-layouts: none -> 5.96 us  [on_device(): jnp.stack([aggregated for _ in range(lax.psum(1, 'feat'))])]
  transfers between devices with their start and end apart: 8 -> 8, of which waited for: 8 -> 8; matrix products, arithmetic and copies ran while one was open for 13% -> 6% of each run, Pallas kernels for 0% -> 0%
where the time goes in v1:
time: 505 us; the launch traced here: 495 us
  waiting for transfers between devices  420 us (83%)
  matrix products  26.3 us (5%)
  starting transfers between devices  25.8 us (5%)
  local copies, waits for them, and re-layouts  16.4 us (3%)
  other arithmetic  6.12 us (1%)
    all_to_all x1, waiting for transfers between devices, on_device(): lax.all_to_all(jnp.stack([aggregated for _ in range(lax.psum(1, 'feat'))]...  360 us
    ppermute x7, waiting for transfers between devices, from_behind(): return lax.ppermute(value, axis, pairs)  59.3 us
    all_to_all x1, starting transfers between devices, on_device(): lax.all_to_all(jnp.stack([aggregated for _ in range(lax.psum(1, 'feat'))]...  23.3 us
    dot_general x8, matrix products, add_source(): jnp.einsum('fsj,sji->fsi', picked, tiles_part, preferred_element_type=jnp...  13.3 us
  transfers between devices with their start and end apart: 8, of which 8 were waited for; matrix products, arithmetic and copies ran while one was open for 6% of the time, Pallas kernels for 0%

profile of v1, /device:TPU:1, one launch (start us, length us, event | category | flops | bytes accessed | tf_op | source)
XLA Modules:
  0.0 494.8 jit_solution(3389323802859677803)
XLA Ops:
  0.0 2.1 collective-permute-start
  2.1 1.2 copy_bitcast_fusion.8
  3.3 1.7 constant_dynamic-slice_fusion
  5.0 0.6 iota_compare_fusion.8
  5.6 0.6 iota_compare_fusion.10
  6.3 0.6 iota_compare_fusion.11
  6.9 0.6 iota_compare_fusion.12
  7.5 0.6 iota_compare_fusion.13
  8.1 0.6 iota_compare_fusion.14
  8.8 0.5 iota_compare_fusion.15
  9.4 1.1 fusion.109
  10.4 1.1 compare_and_fusion
  11.6 0.7 iota_compare_fusion.9
  12.3 0.6 gather_fusion
  12.9 1.7 convolution_bitcast_fusion.7
  14.6 0.4 fusion.19
  15.0 0.9 collective-permute-done
  16.0 0.4 collective-permute-start.1
  16.4 0.1 copy_bitcast_fusion.7
  16.5 0.6 gather_fusion.1
  17.1 1.7 convolution_bitcast_fusion.6
  18.8 0.4 convolution_add_fusion.7
  19.2 10.7 %collective-permute-done.1 = bf16[32,8192]{1,0:T(8,128)(2,1)S(1)} collective-permute-done((bf16[32,8192]{1,0:T(8,128)(2,1)S(1)}, bf16[32,8192]{1,0:T(8,128)(2,1)S(1)}, u32[]{:S(2)}, u32[]{:S(2)}) %collective-permute-start.1) | collective-permute-done | bytes 524320 | tf_op jit(solution)/shard_map/ppermute | solution.py:10
  30.0 0.0 collective-permute-start.2
  30.0 0.1 copy_bitcast_fusion.6
  30.1 0.6 gather_fusion.2
  30.7 1.7 convolution_bitcast_fusion.5
  32.3 0.4 convolution_add_fusion.6
  32.8 10.3 %collective-permute-done.2 = bf16[32,8192]{1,0:T(8,128)(2,1)S(1)} collective-permute-done((bf16[32,8192]{1,0:T(8,128)(2,1)S(1)}, bf16[32,8192]{1,0:T(8,128)(2,1)S(1)}, u32[]{:S(2)}, u32[]{:S(2)}) %collective-permute-start.2) | collective-permute-done | bytes 524320 | tf_op jit(solution)/shard_map/ppermute | solution.py:10
  43.1 0.0 collective-permute-start.3
  43.1 0.1 copy_bitcast_fusion.5
  43.2 0.6 gather_fusion.3
  43.8 1.7 convolution_bitcast_fusion.4
  45.4 0.4 convolution_add_fusion.5
  45.9 9.5 %collective-permute-done.3 = bf16[32,8192]{1,0:T(8,128)(2,1)S(1)} collective-permute-done((bf16[32,8192]{1,0:T(8,128)(2,1)S(1)}, bf16[32,8192]{1,0:T(8,128)(2,1)S(1)}, u32[]{:S(2)}, u32[]{:S(2)}) %collective-permute-start.3) | collective-permute-done | bytes 524320 | tf_op jit(solution)/shard_map/ppermute | solution.py:10
  55.3 0.0 collective-permute-start.4
  55.3 0.1 copy_bitcast_fusion.4
  55.4 0.6 gather_fusion.4
  56.0 1.7 convolution_bitcast_fusion.3
  57.7 0.4 convolution_add_fusion.4
  58.1 8.8 %collective-permute-done.4 = bf16[32,8192]{1,0:T(8,128)(2,1)S(1)} collective-permute-done((bf16[32,8192]{1,0:T(8,128)(2,1)S(1)}, bf16[32,8192]{1,0:T(8,128)(2,1)S(1)}, u32[]{:S(2)}, u32[]{:S(2)}) %collective-permute-start.4) | collective-permute-done | bytes 524320 | tf_op jit(solution)/shard_map/ppermute | solution.py:10
  67.0 0.0 collective-permute-start.5
  67.0 0.1 copy_bitcast_fusion.3
  67.1 0.6 gather_fusion.5
  67.7 1.7 convolution_bitcast_fusion.2
  69.4 0.4 convolution_add_fusion.3
  69.8 9.0 %collective-permute-done.5 = bf16[32,8192]{1,0:T(8,128)(2,1)S(1)} collective-permute-done((bf16[32,8192]{1,0:T(8,128)(2,1)S(1)}, bf16[32,8192]{1,0:T(8,128)(2,1)S(1)}, u32[]{:S(2)}, u32[]{:S(2)}) %collective-permute-start.5) | collective-permute-done | bytes 524320 | tf_op jit(solution)/shard_map/ppermute | solution.py:10
  78.8 0.0 collective-permute-start.6
  78.8 0.1 copy_bitcast_fusion.2
  78.9 0.6 gather_fusion.6
  79.5 1.7 convolution_bitcast_fusion.1
  81.1 0.4 convolution_add_fusion.2
  81.6 10.1 %collective-permute-done.6 = bf16[32,8192]{1,0:T(8,128)(2,1)S(1)} collective-permute-done((bf16[32,8192]{1,0:T(8,128)(2,1)S(1)}, bf16[32,8192]{1,0:T(8,128)(2,1)S(1)}, u32[]{:S(2)}, u32[]{:S(2)}) %collective-permute-start.6) | collective-permute-done | bytes 524320 | tf_op jit(solution)/shard_map/ppermute | solution.py:10
  91.7 0.1 copy_bitcast_fusion.1
  91.8 0.6 gather_fusion.7
  92.4 1.7 convolution_bitcast_fusion
  94.0 0.4 fusion.3
  94.5 0.3 copy.58
  94.8 6.0 %stack.2 = bf16[32,32,8192]{2,1,0:T(8,128)(2,1)} broadcast(bf16[32,8192]{1,0:T(8,128)(2,1)S(1)} %bitcast.123), dimensions={1,2} | broadcast | bytes 17301504 | tf_op jit(solution)/shard_map/stack | solution.py:51
  100.8 23.3 %all-to-all-start = ((bf16[32,32,8192]{2,1,0:T(8,128)(2,1)}), bf16[32,32,8192]{2,1,0:T(8,128)(2,1)}, u32[]{:S(2)}, u32[]{:S(2)}) async-start(bf16[32,32,8192]{2,1,0:T(8,128)(2,1)} %stack.2), calls=%async_computation | async-start | bytes 33554432 | tf_op jit(solution)/shard_map/all_to_all | solution.py:50
  124.1 0.8 dynamic_slice.132
  124.8 360.4 %all-to-all-done = bf16[32,32,8192]{2,1,0:T(8,128)(2,1)} async-done(((bf16[32,32,8192]{2,1,0:T(8,128)(2,1)}), bf16[32,32,8192]{2,1,0:T(8,128)(2,1)}, u32[]{:S(2)}, u32[]{:S(2)}) %all-to-all-start) | async-done | bytes 16777248 | tf_op jit(solution)/shard_map/all_to_all | solution.py:50
  485.2 0.0 copy-done
  485.3 9.6 %fusion.2 = bf16[32,8192]{1,0:T(8,128)(2,1)} fusion(bf16[32,1024]{1,0:T(8,128)(2,1)S(1)} %copy-done, bf16[1024,8192]{1,0:T(8,128)(2,1)} %bitcast.33, f32[32]{0:T(128)S(1)} %dynamic_slice.132), kind=kOutput, calls=%fused_computation.11 | convolution fusion | flops 537657344 | bytes 17367168 | tf_op jit(solution)/shard_map/dot_general | solution.py:47
  (9 shorter events, 0.0 us)
Async XLA Ops:
  0.0 485.2 %copy-start = (bf16[32,1024]{1,0:T(8,128)(2,1)S(1)}, bf16[32,1024]{1,0:T(8,128)(2,1)}, u32[]{:S(2)}) copy-start(bf16[32,1024]{1,0:T(8,128)(2,1)} %param.14) | copy-start | bytes 196612
  0.0 16.0 %collective-permute-start = (bf16[32,8192]{1,0:T(8,128)(2,1)}, bf16[32,8192]{1,0:T(8,128)(2,1)S(1)}, u32[]{:S(2)}, u32[]{:S(2)}) collective-permute-start(bf16[32,8192]{1,0:T(8,128)(2,1)} %param.9), channel_id=1, source_target_pairs={{0,32},{32,64},{64,96},{96,128},{128,160},{160,192},{192,224},{224... | collective-permute-start | bytes 1572872 | tf_op jit(solution)/shard_map/ppermute | solution.py:10
  16.0 14.0 %collective-permute-start.1 = (bf16[32,8192]{1,0:T(8,128)(2,1)S(1)}, bf16[32,8192]{1,0:T(8,128)(2,1)S(1)}, u32[]{:S(2)}, u32[]{:S(2)}) collective-permute-start(bf16[32,8192]{1,0:T(8,128)(2,1)S(1)} %collective-permute-done), channel_id=1, source_target_pairs={{0,32},{32,64},{64,96},{96,128},{128,160},{160,192},{192,224},{224... | collective-permute-start | bytes 1572872 | tf_op jit(solution)/shard_map/ppermute | solution.py:10
  30.0 13.1 %collective-permute-start.2 = (bf16[32,8192]{1,0:T(8,128)(2,1)S(1)}, bf16[32,8192]{1,0:T(8,128)(2,1)S(1)}, u32[]{:S(2)}, u32[]{:S(2)}) collective-permute-start(bf16[32,8192]{1,0:T(8,128)(2,1)S(1)} %collective-permute-done.1), channel_id=1, source_target_pairs={{0,32},{32,64},{64,96},{96,128},{128,160},{160,192},{192,224},{224... | collective-permute-start | bytes 1572872 | tf_op jit(solution)/shard_map/ppermute | solution.py:10
  43.1 12.3 %collective-permute-start.3 = (bf16[32,8192]{1,0:T(8,128)(2,1)S(1)}, bf16[32,8192]{1,0:T(8,128)(2,1)S(1)}, u32[]{:S(2)}, u32[]{:S(2)}) collective-permute-start(bf16[32,8192]{1,0:T(8,128)(2,1)S(1)} %collective-permute-done.2), channel_id=1, source_target_pairs={{0,32},{32,64},{64,96},{96,128},{128,160},{160,192},{192,224},{224... | collective-permute-start | bytes 1572872 | tf_op jit(solution)/shard_map/ppermute | solution.py:10
  55.3 11.6 %collective-permute-start.4 = (bf16[32,8192]{1,0:T(8,128)(2,1)S(1)}, bf16[32,8192]{1,0:T(8,128)(2,1)S(1)}, u32[]{:S(2)}, u32[]{:S(2)}) collective-permute-start(bf16[32,8192]{1,0:T(8,128)(2,1)S(1)} %collective-permute-done.3), channel_id=1, source_target_pairs={{0,32},{32,64},{64,96},{96,128},{128,160},{160,192},{192,224},{224... | collective-permute-start | bytes 1572872 | tf_op jit(solution)/shard_map/ppermute | solution.py:10
  67.0 11.8 %collective-permute-start.5 = (bf16[32,8192]{1,0:T(8,128)(2,1)S(1)}, bf16[32,8192]{1,0:T(8,128)(2,1)S(1)}, u32[]{:S(2)}, u32[]{:S(2)}) collective-permute-start(bf16[32,8192]{1,0:T(8,128)(2,1)S(1)} %collective-permute-done.4), channel_id=1, source_target_pairs={{0,32},{32,64},{64,96},{96,128},{128,160},{160,192},{192,224},{224... | collective-permute-start | bytes 1572872 | tf_op jit(solution)/shard_map/ppermute | solution.py:10
  78.8 12.9 %collective-permute-start.6 = (bf16[32,8192]{1,0:T(8,128)(2,1)S(1)}, bf16[32,8192]{1,0:T(8,128)(2,1)S(1)}, u32[]{:S(2)}, u32[]{:S(2)}) collective-permute-start(bf16[32,8192]{1,0:T(8,128)(2,1)S(1)} %collective-permute-done.5), channel_id=1, source_target_pairs={{0,32},{32,64},{64,96},{96,128},{128,160},{160,192},{192,224},{224... | collective-permute-start | bytes 1572872 | tf_op jit(solution)/shard_map/ppermute | solution.py:10
  100.8 384.5 %all-to-all-start = ((bf16[32,32,8192]{2,1,0:T(8,128)(2,1)}), bf16[32,32,8192]{2,1,0:T(8,128)(2,1)}, u32[]{:S(2)}, u32[]{:S(2)}) async-start(bf16[32,32,8192]{2,1,0:T(8,128)(2,1)} %stack.2), calls=%async_computation | async-start | bytes 33554432 | tf_op jit(solution)/shard_map/all_to_all | solution.py:50
